TPU v7x, 32 devices: a whole 2x2x4 slice. The times are simulated.
32 devices in a mesh: grp: 2 (over y), tm: 4 (over z), height: 4 (over x, core).
Axes of the slice: x: 2, y: 2, z: 4, core: 2. Of those that a mesh axis runs over, the one named last changes fastest.
Arguments:
- latents: bfloat16 [8, 8, 160, 384], P(('grp', 'tm'), 'height'), parts along dimension 0, may hold values from -6 to 6
- gain: float32 [384], replicated, may hold values from 0.1 to 1.9
- bias: float32 [384], replicated, may hold values from -3 to 3
- weight: bfloat16 [10368, 384], replicated, may hold values from -0.0625 to 0.0625
- cotangent: bfloat16 [8, 8, 160, 384], P(('grp', 'tm'), 'height'), parts along dimension 0, may hold values from -6 to 6
Outputs:
- output: bfloat16 [8, 8, 160, 384], P(('grp', 'tm'), 'height'), parts along dimension 0
- latent_grad: bfloat16 [8, 8, 160, 384], P(('grp', 'tm'), 'height'), parts along dimension 0
- weight_grad: float32 [20736, 384], P(('grp', 'tm'), 'height'), parts along dimension 0
There are 2 independent parts, one for each index of `grp`. A program takes and returns all parts, laid end to end along the dimension named above; an argument that names none is the same for every part. Nothing has to cross between parts.
All inputs are finite; a program needn't handle non-finite values.
Results may differ from a plain program's by a relative error of at most 0.0029.
Values may be sent and summed in bfloat16 or wider, within the bound.
No kernel may reach another device: no remote copies, remote signals or barrier semaphores. Data moves between devices by JAX's collectives and lax.ppermute only.
A program may use at most 128 MiB of HBM per device.

v0:
```python
import math
import jax
import jax.numpy as jnp
from jax import lax
from jax.sharding import PartitionSpec as P


def shifted_2(value, axis, by):
    devices = lax.axis_size(axis)
    pairs = [(i, i + by) for i in range(devices) if 0 <= i + by < devices]
    return lax.ppermute(value, axis, pairs)


def padded(cells, sides, width):
    for axis, dim in sides:
        count = lax.axis_size(axis)
        ends = count - 1
        head = lax.slice_in_dim(cells, 0, width, axis=dim)
        tail = lax.slice_in_dim(cells, cells.shape[dim] - width, cells.shape[dim], axis=dim)
        cells = jnp.concatenate(
            [
                lax.ppermute(tail, axis, [(i, (i + 1) % count) for i in range(ends)]),
                cells,
                lax.ppermute(head, axis, [((i + 1) % count, i) for i in range(ends)]),
            ],
            axis=dim,
        )
    return cells


def forward_arrange(cube):
    depth, rows_t, cols_t, inputs, outputs = cube.shape
    return cube.transpose(0, 1, 3, 2, 4).reshape(9, inputs, 3 * outputs)


def backward_arrange(cube):
    depth, rows_t, cols_t, inputs, outputs = cube.shape
    return cube.transpose(0, 1, 4, 2, 3).reshape(9, outputs, 3 * inputs)


def forward_conv(window, cube, row_total, col_total):
    window = window[:, :, : col_total + 2]
    result = lax.conv_general_dilated(
        window[None],
        cube,
        (1, 1, 1),
        "VALID",
        dimension_numbers=("NDHWC", "DHWIO", "NDHWC"),
        preferred_element_type=jnp.float32,
    )
    return result[0, 0]


def backward_conv(window, cube, row_total, col_total):
    window = window[:, :, : col_total + 2]
    result = lax.conv_general_dilated(
        window[None],
        jnp.flip(cube, (0, 1, 2)),
        (1, 1, 1),
        "VALID",
        dimension_numbers=("NDHWC", "DHWOI", "NDHWC"),
        preferred_element_type=jnp.float32,
    )
    return result[0, 0]


def pair_count(tap_rows, share_rows, pair_rows, parts):
    most = 1
    for index in range(parts):
        first = index * share_rows
        last = first + share_rows - 1
        most = max(most, last // pair_rows - first // pair_rows + 1)
    return most


def depth_span(share_rows, tap_rows, channels):
    plane_rows = 9 * channels
    most = 1
    for index in range(tap_rows // share_rows):
        first = index * share_rows
        last = first + share_rows - 1
        most = max(most, last // plane_rows - first // plane_rows + 1)
    return most


def block_weight_grad(framed, cot_all, frame_index, share_rows, channels):
    frame_total, row_total, col_total, slots = cot_all.shape
    plane_rows = 9 * channels
    tap_rows = 27 * channels
    span = depth_span(share_rows, tap_rows, channels)
    first_row = frame_index * share_rows
    first_depth = jnp.minimum(first_row // plane_rows, 3 - span)
    frames = lax.dynamic_slice_in_dim(framed, first_depth, frame_total + span - 1, 0)
    frames = frames[:, :, : col_total + 2]
    terms = lax.conv_general_dilated(
        frames[..., None],
        cot_all[:, :, :, None, :],
        (1, 1, 1),
        "VALID",
        dimension_numbers=("DHWNC", "DHWIO", "DHWNC"),
        preferred_element_type=jnp.float32,
    ).reshape(span * plane_rows, slots)
    return lax.dynamic_slice_in_dim(terms, first_row - first_depth * plane_rows, share_rows, 0)


def gather_rows(own, height_count):
    frame_total, row_count, col_count, channels = own.shape
    height_index = lax.axis_index("height")
    core = height_index % 2
    chip = height_index // 2
    chips = height_count // 2
    first = core == 0
    sibling = [(i, i ^ 1) for i in range(height_count)]
    mine = [own] + [
        lax.ppermute(
            own, "height", [(i, (i + 2 * step) % height_count) for i in range(height_count)]
        )
        for step in range(1, chips)
    ]
    stacked = jnp.concatenate(mine, axis=1)
    twins = lax.ppermute(stacked, "height", sibling)
    block = 2 * row_count
    relative = []
    for step in reversed(range(chips)):
        ours = stacked[:, step * row_count : (step + 1) * row_count]
        theirs = twins[:, step * row_count : (step + 1) * row_count]
        relative.append(
            jnp.where(
                first,
                jnp.concatenate([ours, theirs], axis=1),
                jnp.concatenate([theirs, ours], axis=1),
            )
        )
    relative = jnp.concatenate(relative, axis=1)
    return jnp.concatenate(
        [
            lax.dynamic_slice_in_dim(relative, (place - chip - 1) % chips * block, block, 1)
            for place in range(chips)
        ],
        axis=1,
    )


def local(latents, gain, bias, weight, cotangent):
    frame_count, row_count, col_count, channels = latents.shape
    latent_wide = latents.astype(jnp.float32)
    root_mean = jnp.sqrt(jnp.mean(latent_wide * latent_wide, axis=-1, keepdims=True) + 1e-06)
    normed = latent_wide / root_mean * gain
    hidden = jax.nn.silu(normed).astype(jnp.bfloat16)
    height_count = lax.axis_size("height")
    frame_devices = lax.axis_size("tm")
    frame_index = lax.axis_index("tm")
    row_index = lax.axis_index("height")
    total_rows = row_count * height_count
    total_frames = frame_count * frame_devices
    tap_rows = 27 * channels
    share_rows = tap_rows // frame_devices
    padded_cols = col_count + 2
    right_pad = padded_cols - col_count - 1
    inverse_root = 1.0 / math.sqrt(total_frames * total_rows * col_count)
    weight_cube = weight.reshape(3, 3, 3, channels, channels)
    both_frames = lax.all_gather(
        jnp.concatenate([hidden, cotangent], axis=-1), "tm", axis=0, tiled=True
    )
    hidden_all = gather_rows(both_frames[..., :channels], height_count)
    framed = jnp.pad(hidden_all, ((2, 0), (1, 1), (1, right_pad), (0, 0)))
    cot_frames = both_frames[..., channels:]
    cot_all = lax.all_to_all(cot_frames, "height", split_axis=3, concat_axis=1, tiled=True)
    window = lax.dynamic_slice(
        framed,
        (frame_index * frame_count, row_index * row_count, 0, 0),
        (frame_count + 2, row_count + 2, padded_cols, channels),
    )
    conv_out = forward_conv(window, weight_cube, row_count, col_count).reshape(
        frame_count, row_count, col_count, channels
    )
    output = (latent_wide + conv_out + bias).astype(jnp.bfloat16)
    weight_grad = (
        block_weight_grad(framed, cot_all, frame_index, share_rows, channels) * inverse_root
    )
    cot_future = lax.dynamic_slice_in_dim(
        jnp.pad(cot_frames, ((0, 2), (0, 0), (0, 0), (0, 0))), frame_index * frame_count, 3, 0
    )
    cotangent_edged = padded(cot_future, (("height", 1),), 1)
    future_block = jnp.pad(cotangent_edged, ((0, 0), (0, 0), (1, right_pad), (0, 0)))
    hidden_grad = backward_conv(future_block, weight_cube, row_count, col_count).reshape(
        frame_count, row_count, col_count, channels
    )
    sigmoid_pre = jax.nn.sigmoid(normed)
    normed_grad = hidden_grad * sigmoid_pre * (1.0 + normed * (1.0 - sigmoid_pre))
    scaled_grad = normed_grad * gain
    unit_latent = latent_wide / root_mean
    inner = jnp.mean(scaled_grad * unit_latent, axis=-1, keepdims=True)
    latent_grad = (
        cotangent.astype(jnp.float32) + (scaled_grad - unit_latent * inner) / root_mean
    ).astype(jnp.bfloat16)
    return (output, latent_grad, weight_grad)


def solution(mesh):
    placed = (
        P(("grp", "tm"), "height", None, None),
        P(),
        P(),
        P(),
        P(("grp", "tm"), "height", None, None),
    )
    return jax.shard_map(
        local,
        mesh=mesh,
        in_specs=placed,
        out_specs=(
            P(("grp", "tm"), "height", None, None),
            P(("grp", "tm"), "height", None, None),
            P(("grp", "tm"), "height"),
        ),
        check_vma=False,
    )
```

profile of v0, /device:TPU:0, one launch (start us, length us, event | category | flops | bytes accessed | tf_op | source)
XLA Modules:
  0.0 224.5 jit_solution(6320341675211582955)
XLA Ops:
  7.2 1.1 fusion.49
  8.3 1.2 multiply_convert_fusion
  9.5 1.8 pad_maximum_fusion.3
  11.3 46.4 %all-gather.2.cloned.1.call-done = bf16[4,2,160,768]{3,2,1,0:T(8,128)(2,1)} async-done(((bf16[1,2,160,768]{3,2,1,0:T(8,128)(2,1)}), bf16[4,2,160,768]{3,2,1,0:T(8,128)(2,1)}) %all-gather.2.cloned.1.call-update) | async-done | bytes 1966096 | tf_op jit(solution)/shard_map/all_gather | solution.py:162
  57.7 1.7 fusion.61
  59.4 1.5 collective-permute-start
  61.0 1.0 pad_dynamic-slice_fusion.5
  62.0 1.3 collective-permute-start.3
  63.3 3.8 %collective-permute-start.2 = (bf16[3,1,160,384]{3,2,1,0:T(8,128)(2,1)}, bf16[3,1,160,384]{3,2,1,0:T(8,128)(2,1)}, u32[]{:S(2)}, u32[]{:S(2)}) collective-permute-start(bf16[3,1,160,384]{3,2,1,0:T(8,128)(2,1)} %get-tuple-element.21), channel_id=1, source_target_pairs={{0,1},{1,2},{2,3},{4,5},{5,6},{6,7},{8,9},{9,10},{10,11},{12,13},{... | collective-permute-start | bytes 1105928 | tf_op jit(solution)/shard_map/ppermute | solution.py:22
  67.1 16.1 %collective-permute-done = bf16[4,2,160,384]{3,2,1,0:T(8,128)(2,1)S(1)} collective-permute-done((bf16[4,2,160,384]{3,2,1,0:T(8,128)(2,1)S(1)}, bf16[4,2,160,384]{3,2,1,0:T(8,128)(2,1)S(1)}, u32[]{:S(2)}, u32[]{:S(2)}) %collective-permute-start) | collective-permute-done | bytes 983072 | tf_op jit(solution)/shard_map/ppermute | solution.py:115
  83.1 1.6 pad_maximum_fusion.1
  84.8 2.5 %copy.92 = bf16[4,2,160,384]{2,0,1,3:T(4,128)(2,1)} copy(bf16[4,2,160,384]{3,2,1,0:T(8,128)(2,1)S(1)} %get-tuple-element.17) | data formatting | bytes 1966080 | tf_op jit(solution)/shard_map/slice | solution.py:167
  87.3 3.9 %all-to-all-start = ((bf16[4,2,160,384]{2,0,1,3:T(4,128)(2,1)}), bf16[4,2,160,384]{2,0,1,3:T(4,128)(2,1)S(1)}, u32[]{:S(2)}, u32[]{:S(2)}) async-start(bf16[4,2,160,384]{2,0,1,3:T(4,128)(2,1)} %copy.92), calls=%async_computation | async-start | bytes 3145728 | tf_op jit(solution)/shard_map/all_to_all | solution.py:168
  91.3 1.6 fusion.40
  93.4 0.6 pad.17.clone
  94.3 7.1 %fusion.41 = f32[1,2,8,21,384]{4,2,3,1,0:T(8,128)S(1)} fusion(bf16[3,3,3,384,384]{4,3,2,1,0:T(8,128)(2,1)} %bitcast.52, bf16[3,4,1,7,2,384]{5,3,4,1,0,2:T(8,128)(2,1)S(1)} %slice.34, bf16[3,4,1,8,21,384]{5,3,4,1,0,2:T(8,128)(2,1)S(1)} %copy.89, pred[8,21]{0,1:T(8,128)(4,1)S(1)} %copy-done.7), kind=kOutput, calls=%fused_computation.59 | convolution fusion | flops 2680657920 | bytes 10156200 | tf_op jit(solution)/shard_map/conv_general_dilated | solution.py:56
  102.7 9.1 %all-to-all-done = bf16[4,2,160,384]{2,0,1,3:T(4,128)(2,1)S(1)} async-done(((bf16[4,2,160,384]{2,0,1,3:T(4,128)(2,1)}), bf16[4,2,160,384]{2,0,1,3:T(4,128)(2,1)S(1)}, u32[]{:S(2)}, u32[]{:S(2)}) %all-to-all-start) | async-done | bytes 983072 | tf_op jit(solution)/shard_map/all_to_all | solution.py:168
  111.7 2.5 %copy.94 = bf16[4,4,2,160,96]{4,3,2,1,0:T(8,128)(2,1)} copy(bf16[4,4,2,160,96]{3,0,2,4,1:T(4,128)(2,1)S(1)} %bitcast.46) | data formatting | bytes 1966080 | tf_op jit(solution)/shard_map/all_to_all | solution.py:168
  114.3 1.7 fusion.62
  116.3 0.8 copy-done.3
  117.5 1.6 fusion.20
  119.2 5.8 %fusion.10 = bf16[6,10,162,384]{3,2,1,0:T(8,128)(2,1)S(1)} fusion(bf16[4,4,160,384]{3,2,1,0:T(8,128)(2,1)S(1)} %get-tuple-element.16, bf16[4,4,160,384]{3,2,1,0:T(8,128)(2,1)S(1)} %get-tuple-element.15), kind=kLoop, calls=%fused_computation.15 | loop fusion | flops 70917120 | bytes 11397120 | tf_op jit(solution)/shard_map/concatenate | solution.py:135
  125.8 0.6 pad.15.clone
  127.1 3.8 %fusion.44 = f32[1,2,8,21,384]{4,2,3,1,0:T(8,128)S(1)} fusion(bf16[3,3,3,384,384]{4,3,2,1,0:T(8,128)(2,1)S(1)} %bitcast.55, bf16[3,4,1,7,2,384]{5,3,4,1,0,2:T(8,128)(2,1)S(1)} %slice.31, bf16[3,4,1,8,21,384]{5,3,4,1,0,2:T(8,128)(2,1)S(1)} %copy.84, pred[8,21]{0,1:T(8,128)(4,1)S(1)} %copy-done.7), kind=kOutput, calls=%fused_computation.60 | convolution fusion | flops 2680657920 | bytes 10156200 | tf_op jit(solution)/shard_map/conv_general_dilated | solution.py:43
  131.2 1.0 slice.32
  132.1 0.6 dynamic-slice_bitcast_fusion
  132.8 0.7 copy-done.4
  133.5 74.5 %fusion.6 = f32[2,3,3,384,96]{3,4,2,1,0:T(8,128)S(1)} fusion(bf16[5,10,162,384,1]{3,2,1,0,4:T(8,128)(2,1)S(1)} %dynamic-slice_bitcast_fusion, bf16[4,8,160,1,96]{4,2,1,0,3:T(8,128)(2,1)S(1)} %bitcast.51), kind=kOutput, calls=%fused_computation.11 | convolution fusion | flops 6794772480 | bytes 9858048 | tf_op jit(solution)/shard_map/conv_general_dilated | solution.py:95
  207.9 1.8 copy.97
  209.8 2.8 %reshape.42 = f32[6912,96]{0,1:T(8,128)} reshape(f32[2,3,3,384,96]{3,2,1,0,4:T(4,128)S(1)} %copy.97) | data formatting | bytes 5308416 | tf_op jit(solution)/shard_map/reshape | solution.py:102
  212.6 2.5 %dynamic-slice_multiply_fusion = f32[2592,96]{0,1:T(8,128)} fusion(f32[6912,96]{0,1:T(8,128)} %reshape.42, s32[]{:T(128)S(6)} %select_n.66), kind=kLoop, calls=%fused_computation.61 | loop fusion | flops 248832 | bytes 1990660 | tf_op jit(solution)/shard_map/mul | solution.py:179
  215.1 2.6 %add_convert_fusion = (bf16[1,2,160,384]{3,2,1,0:T(8,128)(2,1)}, bf16[1,2,160,384]{3,2,1,0:T(8,128)(2,1)}) fusion(bf16[1,2,160,384]{3,2,1,0:T(8,128)(2,1)} %param.9, f32[2,160]{1,0:T(2,128)S(1)} %broadcast_multiply_fusion, f32[2,160]{1,0:T(2,128)S(1)} %add_sqrt_fusion, f32[384]{0:T(512)S(1)} %copy-done.5, f32[1,2,1,160,384]{4,1,3,2,0:T(2,128)} %copy-done, ...), kind=kLoop, calls=%fused_computation.76 | loop fusion | flops 2580480 | bytes 1971712 | tf_op jit(solution)/shard_map/convert_element_type | solution.py:196
  (41 shorter events, 4.7 us)
Async XLA Ops:
  7.2 50.6 %all-gather.2.cloned.1.call-start = ((), (), s32[]{:S(2)}) async-start(), calls=%async_computation.1 | async-start | bytes 2457600 | tf_op jit(solution)/shard_map/all_gather | solution.py:162
  59.4 23.7 %collective-permute-start = (bf16[4,2,160,384]{3,2,1,0:T(8,128)(2,1)S(1)}, bf16[4,2,160,384]{3,2,1,0:T(8,128)(2,1)S(1)}, u32[]{:S(2)}, u32[]{:S(2)}) collective-permute-start(bf16[4,2,160,384]{3,2,1,0:T(8,128)(2,1)S(1)} %get-tuple-element.18), channel_id=1, source_target_pairs={{0,2},{1,3},{2,0},{3,1},{4,6},{5,7},{6,4},{7,5},{8,10},{9,11},{10,... | collective-permute-start | bytes 2949128 | tf_op jit(solution)/shard_map/ppermute | solution.py:115
  62.0 29.3 %collective-permute-start.3 = (bf16[3,1,160,384]{3,2,1,0:T(8,128)(2,1)}, bf16[3,1,160,384]{3,2,1,0:T(8,128)(2,1)}, u32[]{:S(2)}, u32[]{:S(2)}) collective-permute-start(bf16[3,1,160,384]{3,2,1,0:T(8,128)(2,1)} %get-tuple-element.22), channel_id=1, source_target_pairs={{1,0},{2,1},{3,2},{5,4},{6,5},{7,6},{9,8},{10,9},{11,10},{13,12},{... | collective-permute-start | bytes 1105928 | tf_op jit(solution)/shard_map/ppermute | solution.py:24
  63.3 28.0 %collective-permute-start.2 = (bf16[3,1,160,384]{3,2,1,0:T(8,128)(2,1)}, bf16[3,1,160,384]{3,2,1,0:T(8,128)(2,1)}, u32[]{:S(2)}, u32[]{:S(2)}) collective-permute-start(bf16[3,1,160,384]{3,2,1,0:T(8,128)(2,1)} %get-tuple-element.21), channel_id=1, source_target_pairs={{0,1},{1,2},{2,3},{4,5},{5,6},{6,7},{8,9},{9,10},{10,11},{12,13},{... | collective-permute-start | bytes 1105928 | tf_op jit(solution)/shard_map/ppermute | solution.py:22
  83.1 4.2 %copy-start.2 = (bf16[4,2,160,384]{3,2,1,0:T(8,128)(2,1)}, bf16[4,2,160,384]{3,2,1,0:T(8,128)(2,1)S(1)}, u32[]{:S(2)}) copy-start(bf16[4,2,160,384]{3,2,1,0:T(8,128)(2,1)S(1)} %collective-permute-done) | copy-start | bytes 2949124
  84.7 29.5 %collective-permute-start.1 = (bf16[4,4,160,384]{3,2,1,0:T(8,128)(2,1)}, bf16[4,4,160,384]{3,2,1,0:T(8,128)(2,1)}, u32[]{:S(2)}, u32[]{:S(2)}) collective-permute-start(bf16[4,4,160,384]{3,2,1,0:T(8,128)(2,1)} %pad_maximum_fusion.1), channel_id=1, source_target_pairs={{0,1},{1,0},{2,3},{3,2},{4,5},{5,4},{6,7},{7,6},{8,9},{9,8},{10,11... | collective-permute-start | bytes 5898248 | tf_op jit(solution)/shard_map/ppermute | solution.py:121
  87.3 24.4 %all-to-all-start = ((bf16[4,2,160,384]{2,0,1,3:T(4,128)(2,1)}), bf16[4,2,160,384]{2,0,1,3:T(4,128)(2,1)S(1)}, u32[]{:S(2)}, u32[]{:S(2)}) async-start(bf16[4,2,160,384]{2,0,1,3:T(4,128)(2,1)} %copy.92), calls=%async_computation | async-start | bytes 3145728 | tf_op jit(solution)/shard_map/all_to_all | solution.py:168
  93.4 0.9 copy-start.7
  94.3 7.6 %copy-start.1 = (bf16[1,2,160,384]{3,2,1,0:T(8,128)(2,1)S(1)}, bf16[1,2,160,384]{3,2,1,0:T(8,128)(2,1)}, u32[]{:S(2)}) copy-start(bf16[1,2,160,384]{3,2,1,0:T(8,128)(2,1)} %param.5) | copy-start | bytes 737284
  94.3 7.6 %copy-start.5 = (f32[384]{0:T(512)S(1)}, f32[384]{0:T(512)}, u32[]{:S(2)}) copy-start(f32[384]{0:T(512)} %param.6) | copy-start | bytes 4612
  101.9 0.8 copy-start
  116.0 1.2 copy-start.3
  119.2 7.5 %slice-start = ((s8[7962624]{0:T(1024)(128)(4,1)}), s8[4194304]{0:T(1024)(128)(4,1)S(1)}, s32[]{:S(2)}) async-start(s8[7962624]{0:T(1024)(128)(4,1)} %bitcast.53), calls=%async_computation.2 | async-start | bytes 8388608
  125.0 2.1 slice-start.1
  132.1 1.3 copy-start.4
  209.7 5.3 %copy-start.6 = (f32[384]{0:T(512)S(1)}, f32[384]{0:T(512)}, u32[]{:S(2)}) copy-start(f32[384]{0:T(512)} %param.7) | copy-start | bytes 4612
Sparse Core Ops, SparseCore 0:
  11.4 46.2 all-gather.1
where the time goes:
time: 225 us; the launch traced here: 224 us
  matrix products  85.4 us (38%)
  waiting for transfers between devices  71.6 us (32%)
  local copies, waits for them, and re-layouts  21.8 us (10%)
  other arithmetic  20.9 us (9%)
  between operations  14.3 us (6%)
  starting transfers between devices  10.5 us (5%)
    conv_general_dilated x1, matrix products, block_weight_grad(): lax.conv_general_dilated(frames[..., None], cot_all[:, :, :, None, :], (1...  74.5 us
    all_gather x1, waiting for transfers between devices, local(): lax.all_gather(jnp.concatenate([hidden, cotangent], axis=-1), 'tm', axis=...  46.4 us
    ppermute x1, waiting for transfers between devices, gather_rows(): lax.ppermute(own, 'height', [(i, (i + 2 * step) % height_count) for i in...  16.1 us
    all_to_all x1, waiting for transfers between devices, local(): lax.all_to_all(cot_frames, 'height', split_axis=3, concat_axis=1, tiled=T...  9.06 us
    conv_general_dilated x1, matrix products, backward_conv(): lax.conv_general_dilated(window[None], jnp.flip(cube, (0, 1, 2)), (1, 1,...  7.08 us
    concatenate x1, other arithmetic, gather_rows(): jnp.concatenate([lax.dynamic_slice_in_dim(relative, (place - chip - 1) %...  5.81 us
  transfers between devices with their start and end apart: 6, of which 3 were waited for; matrix products, arithmetic and copies ran while one was open for 8% of the time, Pallas kernels for 0%

commit v1 on v0

--- a/solution.py
+++ b/solution.py
@@ -3,6 +3,29 @@
 import jax.numpy as jnp
 from jax import lax
 from jax.sharding import PartitionSpec as P
+
+
+def _find_record(view, axis_tag, d0):
+    f_now = lax.axis_size(axis_tag)
+    val2, vec_out, r_now = (f_now, lax.axis_index(axis_tag), view.shape[d0])
+    heard = jnp.zeros(
+        tuple((b * val2 if dev == d0 else b for dev, b in enumerate(view.shape))), view.dtype
+    )
+    new = lax.dynamic_update_slice_in_dim(heard, view, vec_out * r_now, axis=d0)
+    now = reply = view
+    i0 = 1
+    while i0 < val2 // 2 + 1:
+        near = tuple(((dev, (dev + 1) % val2) for dev in range(val2)))
+        now = lax.ppermute(now, axis_tag, perm=near)
+        new = lax.dynamic_update_slice_in_dim(new, now, (vec_out - i0) % val2 * r_now, axis=d0)
+        if 2 * i0 < val2:
+            fresh = tuple(((dev, (dev - 1) % val2) for dev in range(val2)))
+            reply = lax.ppermute(reply, axis_tag, fresh)
+            new = lax.dynamic_update_slice_in_dim(
+                new, reply, (vec_out + i0) % val2 * r_now, axis=d0
+            )
+        i0 += 1
+    return new
 
 
 def shifted_2(value, axis, by):
@@ -159,9 +182,7 @@
     right_pad = padded_cols - col_count - 1
     inverse_root = 1.0 / math.sqrt(total_frames * total_rows * col_count)
     weight_cube = weight.reshape(3, 3, 3, channels, channels)
-    both_frames = lax.all_gather(
-        jnp.concatenate([hidden, cotangent], axis=-1), "tm", axis=0, tiled=True
-    )
+    both_frames = _find_record(jnp.concatenate([hidden, cotangent], axis=-1), "tm", 0)
     hidden_all = gather_rows(both_frames[..., :channels], height_count)
     framed = jnp.pad(hidden_all, ((2, 0), (1, 1), (1, right_pad), (0, 0)))
     cot_frames = both_frames[..., channels:]

time: 225 us -> 207 us (0.920)
  waiting for transfers between devices: 71.6 us -> 55.2 us
  between operations: 14.3 us -> 0.97 us
  local copies, waits for them, and re-layouts: 21.8 us -> 29.9 us
  starting transfers between devices: 10.5 us -> 15.6 us
    all_gather x1 -> x0, waiting for transfers between devices: 46.4 us -> none  [local(): lax.all_gather(jnp.concatenate([hidden, cotangent], axis=-1), 'tm', axis=...]
    ppermute x0 -> x3, waiting for transfers between devices: none -> 30.7 us  [the longest x2 22.3 us: _find_record(): now = lax.ppermute(now, axis_tag, perm=near)]
    ppermute x0 -> x3, starting transfers between devices: none -> 5.07 us  [the longest x2 3.01 us: _find_record(): now = lax.ppermute(now, axis_tag, perm=near)]
    all_to_all x1 -> x2, local copies, waits for them, and re-layouts: 2.54 us -> 5.96 us  [local(): lax.all_to_all(cot_frames, 'height', split_axis=3, concat_axis=1, tiled=T...]
    dynamic_update_slice x0 -> x3, local copies, waits for them, and re-layouts: none -> 2.48 us  [the longest x2 1.67 us: _find_record(): lax.dynamic_update_slice_in_dim(new, now, (vec_out - i0) % val2 * r_now,...]
  transfers between devices with their start and end apart: 6 -> 8, of which waited for: 3 -> 5; matrix products, arithmetic and copies ran while one was open for 8% -> 12% of each run, Pallas kernels for 0% -> 0%
where the time goes in v1:
time: 207 us; the launch traced here: 206 us
  matrix products  85.7 us (41%)
  waiting for transfers between devices  55.2 us (27%)
  local copies, waits for them, and re-layouts  29.9 us (14%)
  other arithmetic  18.8 us (9%)
  starting transfers between devices  15.6 us (8%)
    conv_general_dilated x1, matrix products, block_weight_grad(): lax.conv_general_dilated(frames[..., None], cot_all[:, :, :, None, :], (1...  74.8 us
    ppermute x2, waiting for transfers between devices, _find_record(): now = lax.ppermute(now, axis_tag, perm=near)  22.3 us
    ppermute x1, waiting for transfers between devices, gather_rows(): lax.ppermute(own, 'height', [(i, (i + 2 * step) % height_count) for i in...  16.1 us
    all_to_all x1, waiting for transfers between devices, local(): lax.all_to_all(cot_frames, 'height', split_axis=3, concat_axis=1, tiled=T...  8.42 us
    ppermute x1, waiting for transfers between devices, _find_record(): reply = lax.ppermute(reply, axis_tag, fresh)  8.4 us
    conv_general_dilated x1, matrix products, backward_conv(): lax.conv_general_dilated(window[None], jnp.flip(cube, (0, 1, 2)), (1, 1,...  7.03 us
    all_to_all x2, local copies, waits for them, and re-layouts, local(): lax.all_to_all(cot_frames, 'height', split_axis=3, concat_axis=1, tiled=T...  5.96 us
    concatenate x1, other arithmetic, gather_rows(): jnp.concatenate([lax.dynamic_slice_in_dim(relative, (place - chip - 1) %...  5.85 us
  transfers between devices with their start and end apart: 8, of which 5 were waited for; matrix products, arithmetic and copies ran while one was open for 12% of the time, Pallas kernels for 0%

profile of v1, /device:TPU:0, one launch (start us, length us, event | category | flops | bytes accessed | tf_op | source)
XLA Modules:
  0.0 206.2 jit_solution(17440413600158368)
XLA Ops:
  0.6 1.1 fusion.49
  1.8 1.2 multiply_convert_fusion
  3.0 1.4 broadcast_in_dim.20
  5.3 3.0 %collective-permute-start = (bf16[1,2,160,768]{3,2,1,0:T(8,128)(2,1)S(1)}, bf16[1,2,160,768]{3,2,1,0:T(8,128)(2,1)S(1)}, u32[]{:S(2)}, u32[]{:S(2)}) collective-permute-start(bf16[1,2,160,768]{3,2,1,0:T(8,128)(2,1)S(1)} %get-tuple-element.14), channel_id=1, source_target_pairs={{0,4},{4,8},{8,12},{12,0},{1,5},{5,9},{9,13},{13,1},{2,6},{6,10},{... | collective-permute-start | bytes 1474568 | tf_op jit(solution)/shard_map/ppermute | solution.py:19
  8.3 2.1 collective-permute-start.1
  10.4 12.1 %collective-permute-done = bf16[1,2,160,768]{3,2,1,0:T(8,128)(2,1)S(1)} collective-permute-done((bf16[1,2,160,768]{3,2,1,0:T(8,128)(2,1)S(1)}, bf16[1,2,160,768]{3,2,1,0:T(8,128)(2,1)S(1)}, u32[]{:S(2)}, u32[]{:S(2)}) %collective-permute-start) | collective-permute-done | bytes 491552 | tf_op jit(solution)/shard_map/ppermute | solution.py:19
  23.3 8.4 %collective-permute-done.1 = bf16[1,2,160,768]{3,2,1,0:T(8,128)(2,1)S(1)} collective-permute-done((bf16[1,2,160,768]{3,2,1,0:T(8,128)(2,1)S(1)}, bf16[1,2,160,768]{3,2,1,0:T(8,128)(2,1)S(1)}, u32[]{:S(2)}, u32[]{:S(2)}) %collective-permute-start.1) | collective-permute-done | bytes 491552 | tf_op jit(solution)/shard_map/ppermute | solution.py:23
  32.5 10.2 %collective-permute-done.2 = bf16[1,2,160,768]{3,2,1,0:T(8,128)(2,1)S(1)} collective-permute-done((bf16[1,2,160,768]{3,2,1,0:T(8,128)(2,1)S(1)}, bf16[1,2,160,768]{3,2,1,0:T(8,128)(2,1)S(1)}, u32[]{:S(2)}, u32[]{:S(2)}) %collective-permute-start.2) | collective-permute-done | bytes 491552 | tf_op jit(solution)/shard_map/ppermute | solution.py:19
  43.5 1.7 fusion.61
  45.2 1.6 collective-permute-start.3
  46.8 1.0 pad_dynamic-slice_fusion.5
  47.8 1.3 collective-permute-start.6
  49.1 3.8 %collective-permute-start.5 = (bf16[3,1,160,384]{3,2,1,0:T(8,128)(2,1)}, bf16[3,1,160,384]{3,2,1,0:T(8,128)(2,1)}, u32[]{:S(2)}, u32[]{:S(2)}) collective-permute-start(bf16[3,1,160,384]{3,2,1,0:T(8,128)(2,1)} %get-tuple-element.12), channel_id=1, source_target_pairs={{0,1},{1,2},{2,3},{4,5},{5,6},{6,7},{8,9},{9,10},{10,11},{12,13},{... | collective-permute-start | bytes 1105928 | tf_op jit(solution)/shard_map/ppermute | solution.py:45
  52.9 16.1 %collective-permute-done.3 = bf16[4,2,160,384]{3,2,1,0:T(8,128)(2,1)S(1)} collective-permute-done((bf16[4,2,160,384]{3,2,1,0:T(8,128)(2,1)S(1)}, bf16[4,2,160,384]{3,2,1,0:T(8,128)(2,1)S(1)}, u32[]{:S(2)}, u32[]{:S(2)}) %collective-permute-start.3) | collective-permute-done | bytes 983072 | tf_op jit(solution)/shard_map/ppermute | solution.py:138
  69.0 1.6 pad_maximum_fusion.1
  70.6 3.0 %copy.52 = bf16[4,2,160,384]{2,1,0,3:T(2,128)(2,1)} copy(bf16[4,2,160,384]{3,2,1,0:T(8,128)(2,1)S(1)} %get-tuple-element.8) | data formatting | bytes 1966080 | tf_op jit(solution)/shard_map/slice | solution.py:188
  73.7 3.9 %all-to-all-start = ((bf16[4,2,160,384]{2,1,0,3:T(2,128)(2,1)}), bf16[4,2,160,384]{2,1,0,3:T(2,128)(2,1)S(1)}, u32[]{:S(2)}, u32[]{:S(2)}) async-start(bf16[4,2,160,384]{2,1,0,3:T(2,128)(2,1)} %copy.52), calls=%async_computation | async-start | bytes 3145728 | tf_op jit(solution)/shard_map/all_to_all | solution.py:189
  77.7 1.6 fusion.40
  81.1 7.0 %fusion.41 = f32[1,2,8,21,384]{4,2,3,1,0:T(8,128)S(1)} fusion(bf16[3,3,3,384,384]{4,3,2,1,0:T(8,128)(2,1)} %bitcast.51, bf16[3,4,1,7,2,384]{5,3,4,1,0,2:T(8,128)(2,1)S(1)} %slice.34, bf16[3,4,1,8,21,384]{5,3,4,1,0,2:T(8,128)(2,1)S(1)} %copy.49, pred[8,21]{0,1:T(8,128)(4,1)S(1)} %copy-done.11), kind=kOutput, calls=%fused_computation.59 | convolution fusion | flops 2680657920 | bytes 10156200 | tf_op jit(solution)/shard_map/conv_general_dilated | solution.py:79
  89.9 8.4 %all-to-all-done = bf16[4,2,160,384]{2,1,0,3:T(2,128)(2,1)S(1)} async-done(((bf16[4,2,160,384]{2,1,0,3:T(2,128)(2,1)}), bf16[4,2,160,384]{2,1,0,3:T(2,128)(2,1)S(1)}, u32[]{:S(2)}, u32[]{:S(2)}) %all-to-all-start) | async-done | bytes 983072 | tf_op jit(solution)/shard_map/all_to_all | solution.py:189
  98.3 4.4 %copy.58 = bf16[4,2,160,4,96]{4,3,2,1,0:T(4,128)(2,1)} copy(bf16[4,2,160,4,96]{2,1,0,4,3:T(2,128)(2,1)S(1)} %bitcast.44) | data formatting | bytes 1966080 | tf_op jit(solution)/shard_map/all_to_all | solution.py:189
  102.7 1.5 copy.54
  104.2 1.7 fusion.62
  107.5 1.6 fusion.20
  109.2 5.9 %fusion.10 = bf16[6,10,162,384]{3,2,1,0:T(8,128)(2,1)S(1)} fusion(bf16[4,4,160,384]{3,2,1,0:T(8,128)(2,1)S(1)} %get-tuple-element.7, bf16[4,4,160,384]{3,2,1,0:T(8,128)(2,1)S(1)} %get-tuple-element.6), kind=kLoop, calls=%fused_computation.15 | loop fusion | flops 70917120 | bytes 11397120 | tf_op jit(solution)/shard_map/concatenate | solution.py:158
  117.1 3.9 %fusion.44 = f32[1,2,8,21,384]{4,2,3,1,0:T(8,128)S(1)} fusion(bf16[3,3,3,384,384]{4,3,2,1,0:T(8,128)(2,1)S(1)} %bitcast.54, bf16[3,4,1,7,2,384]{5,3,4,1,0,2:T(8,128)(2,1)S(1)} %slice.31, bf16[3,4,1,8,21,384]{5,3,4,1,0,2:T(8,128)(2,1)S(1)} %copy.44, pred[8,21]{0,1:T(8,128)(4,1)S(1)} %copy-done.11), kind=kOutput, calls=%fused_computation.60 | convolution fusion | flops 2680657920 | bytes 10156200 | tf_op jit(solution)/shard_map/conv_general_dilated | solution.py:66
  121.2 1.0 slice.32
  122.8 74.8 %fusion.6 = f32[2,3,3,384,96]{3,4,2,1,0:T(8,128)S(1)} fusion(bf16[5,10,162,384,1]{3,2,1,0,4:T(8,128)(2,1)S(1)} %dynamic-slice_bitcast_fusion, bf16[4,8,160,1,96]{4,2,1,0,3:T(8,128)(2,1)S(1)} %bitcast.50), kind=kOutput, calls=%fused_computation.11 | convolution fusion | flops 6794772480 | bytes 9858048 | tf_op jit(solution)/shard_map/conv_general_dilated | solution.py:118
  197.6 1.8 copy.57
  199.4 2.8 %reshape.42 = f32[6912,96]{0,1:T(8,128)} reshape(f32[2,3,3,384,96]{3,2,1,0,4:T(4,128)S(1)} %copy.57) | data formatting | bytes 5308416 | tf_op jit(solution)/shard_map/reshape | solution.py:125
  202.3 2.6 %dynamic-slice_multiply_fusion = f32[2592,96]{0,1:T(8,128)} fusion(f32[6912,96]{0,1:T(8,128)} %reshape.42, s32[]{:T(128)S(6)} %select_n.97), kind=kLoop, calls=%fused_computation.61 | loop fusion | flops 248832 | bytes 1990660 | tf_op jit(solution)/shard_map/mul | solution.py:200
  205.0 1.2 add_convert_fusion
  (57 shorter events, 11.5 us)
Async XLA Ops:
  0.6 3.8 %copy-start.7 = (bf16[1,2,160,384]{3,2,1,0:T(8,128)(2,1)S(1)}, bf16[1,2,160,384]{3,2,1,0:T(8,128)(2,1)}, u32[]{:S(2)}) copy-start(bf16[1,2,160,384]{3,2,1,0:T(8,128)(2,1)} %param.9) | copy-start | bytes 737284
  5.3 17.2 %collective-permute-start = (bf16[1,2,160,768]{3,2,1,0:T(8,128)(2,1)S(1)}, bf16[1,2,160,768]{3,2,1,0:T(8,128)(2,1)S(1)}, u32[]{:S(2)}, u32[]{:S(2)}) collective-permute-start(bf16[1,2,160,768]{3,2,1,0:T(8,128)(2,1)S(1)} %get-tuple-element.14), channel_id=1, source_target_pairs={{0,4},{4,8},{8,12},{12,0},{1,5},{5,9},{9,13},{13,1},{2,6},{6,10},{... | collective-permute-start | bytes 1474568 | tf_op jit(solution)/shard_map/ppermute | solution.py:19
  8.3 23.4 %collective-permute-start.1 = (bf16[1,2,160,768]{3,2,1,0:T(8,128)(2,1)S(1)}, bf16[1,2,160,768]{3,2,1,0:T(8,128)(2,1)S(1)}, u32[]{:S(2)}, u32[]{:S(2)}) collective-permute-start(bf16[1,2,160,768]{3,2,1,0:T(8,128)(2,1)S(1)} %get-tuple-element.14), channel_id=1, source_target_pairs={{0,12},{4,0},{8,4},{12,8},{1,13},{5,1},{9,5},{13,9},{2,14},{6,2},{... | collective-permute-start | bytes 1474568 | tf_op jit(solution)/shard_map/ppermute | solution.py:23
  22.5 20.2 %collective-permute-start.2 = (bf16[1,2,160,768]{3,2,1,0:T(8,128)(2,1)S(1)}, bf16[1,2,160,768]{3,2,1,0:T(8,128)(2,1)S(1)}, u32[]{:S(2)}, u32[]{:S(2)}) collective-permute-start(bf16[1,2,160,768]{3,2,1,0:T(8,128)(2,1)S(1)} %collective-permute-done), channel_id=1, source_target_pairs={{0,4},{4,8},{8,12},{12,0},{1,5},{5,9},{9,13},{13,1},{2,6},{6,10},{... | collective-permute-start | bytes 1474568 | tf_op jit(solution)/shard_map/ppermute | solution.py:19
  45.2 23.8 %collective-permute-start.3 = (bf16[4,2,160,384]{3,2,1,0:T(8,128)(2,1)S(1)}, bf16[4,2,160,384]{3,2,1,0:T(8,128)(2,1)S(1)}, u32[]{:S(2)}, u32[]{:S(2)}) collective-permute-start(bf16[4,2,160,384]{3,2,1,0:T(8,128)(2,1)S(1)} %get-tuple-element.9), channel_id=1, source_target_pairs={{0,2},{1,3},{2,0},{3,1},{4,6},{5,7},{6,4},{7,5},{8,10},{9,11},{10,... | collective-permute-start | bytes 2949128 | tf_op jit(solution)/shard_map/ppermute | solution.py:138
  47.8 29.9 %collective-permute-start.6 = (bf16[3,1,160,384]{3,2,1,0:T(8,128)(2,1)}, bf16[3,1,160,384]{3,2,1,0:T(8,128)(2,1)}, u32[]{:S(2)}, u32[]{:S(2)}) collective-permute-start(bf16[3,1,160,384]{3,2,1,0:T(8,128)(2,1)} %get-tuple-element.13), channel_id=1, source_target_pairs={{1,0},{2,1},{3,2},{5,4},{6,5},{7,6},{9,8},{10,9},{11,10},{13,12},{... | collective-permute-start | bytes 1105928 | tf_op jit(solution)/shard_map/ppermute | solution.py:47
  49.1 28.6 %collective-permute-start.5 = (bf16[3,1,160,384]{3,2,1,0:T(8,128)(2,1)}, bf16[3,1,160,384]{3,2,1,0:T(8,128)(2,1)}, u32[]{:S(2)}, u32[]{:S(2)}) collective-permute-start(bf16[3,1,160,384]{3,2,1,0:T(8,128)(2,1)} %get-tuple-element.12), channel_id=1, source_target_pairs={{0,1},{1,2},{2,3},{4,5},{5,6},{6,7},{8,9},{9,10},{10,11},{12,13},{... | collective-permute-start | bytes 1105928 | tf_op jit(solution)/shard_map/ppermute | solution.py:45
  69.0 1.6 copy-start.4
  70.6 33.6 %collective-permute-start.4 = (bf16[4,4,160,384]{3,2,1,0:T(8,128)(2,1)}, bf16[4,4,160,384]{3,2,1,0:T(8,128)(2,1)}, u32[]{:S(2)}, u32[]{:S(2)}) collective-permute-start(bf16[4,4,160,384]{3,2,1,0:T(8,128)(2,1)} %pad_maximum_fusion.1), channel_id=1, source_target_pairs={{0,1},{1,0},{2,3},{3,2},{4,5},{5,4},{6,7},{7,6},{8,9},{9,8},{10,11... | collective-permute-start | bytes 5898248 | tf_op jit(solution)/shard_map/ppermute | solution.py:144
  73.7 24.6 %all-to-all-start = ((bf16[4,2,160,384]{2,1,0,3:T(2,128)(2,1)}), bf16[4,2,160,384]{2,1,0,3:T(2,128)(2,1)S(1)}, u32[]{:S(2)}, u32[]{:S(2)}) async-start(bf16[4,2,160,384]{2,1,0,3:T(2,128)(2,1)} %copy.52), calls=%async_computation | async-start | bytes 3145728 | tf_op jit(solution)/shard_map/all_to_all | solution.py:189
  80.4 0.7 copy-start.11
  88.1 0.9 copy-start.2
  88.1 0.9 copy-start.9
  89.1 0.8 copy-start
  106.0 1.2 copy-start.5
  109.1 7.5 %slice-start = ((s8[7962624]{0:T(1024)(128)(4,1)}), s8[4194304]{0:T(1024)(128)(4,1)S(1)}, s32[]{:S(2)}) async-start(s8[7962624]{0:T(1024)(128)(4,1)} %bitcast.52), calls=%async_computation.1 | async-start | bytes 8388608
  115.0 2.1 %slice-start.1 = ((s8[7962624]{0:T(1024)(128)(4,1)}), s8[3768320]{0:T(1024)(128)(4,1)S(1)}, s32[]{:S(2)}) async-start(s8[7962624]{0:T(1024)(128)(4,1)} %bitcast.52), calls=%async_computation.2 | async-start | bytes 7536640
  202.3 2.7 %copy-start.1 = (f32[1,2,1,160,384]{4,1,3,2,0:T(2,128)S(1)}, f32[1,2,1,160,384]{4,1,3,2,0:T(2,128)}, u32[]{:S(2)}) copy-start(f32[1,2,1,160,384]{4,1,3,2,0:T(2,128)} %copy-done) | copy-start | bytes 1474564
  202.3 2.7 %copy-start.3 = (bf16[1,2,160,384]{3,2,1,0:T(8,128)(2,1)S(1)}, bf16[1,2,160,384]{3,2,1,0:T(8,128)(2,1)}, u32[]{:S(2)}) copy-start(bf16[1,2,160,384]{3,2,1,0:T(8,128)(2,1)} %param.5) | copy-start | bytes 737284
  202.3 2.7 %copy-start.6 = (f32[1,2,1,160,384]{4,1,3,2,0:T(2,128)S(1)}, f32[1,2,1,160,384]{4,1,3,2,0:T(2,128)}, u32[]{:S(2)}) copy-start(f32[1,2,1,160,384]{4,1,3,2,0:T(2,128)} %slice.32) | copy-start | bytes 1474564
  202.3 2.7 %copy-start.8 = (bf16[1,2,160,384]{3,2,1,0:T(8,128)(2,1)S(1)}, bf16[1,2,160,384]{3,2,1,0:T(8,128)(2,1)}, u32[]{:S(2)}) copy-start(bf16[1,2,160,384]{3,2,1,0:T(8,128)(2,1)} %param.9) | copy-start | bytes 737284
  202.3 2.7 %copy-start.10 = (f32[384]{0:T(512)S(1)}, f32[384]{0:T(512)}, u32[]{:S(2)}) copy-start(f32[384]{0:T(512)} %param.7) | copy-start | bytes 4612
